TPU v7x, 256 devices: a whole 4x4x8 slice. The times are simulated.
256 devices in a mesh: row: 4 (over y), col: 16 (over z_hi, x, core), dep: 4 (over z_lo).
Axes of the slice: x: 4, y: 4, z: 8 (z_hi: 2, z_lo: 4; z = z_hi * 4 + z_lo), core: 2. Of those that a mesh axis runs over, the one named last changes fastest.
Arguments:
- grad_out: bfloat16 [4, 512, 12288], P('row', 'dep', 'col'), may hold values from -7 to 7
- out_weight: bfloat16 [8192, 12288], P('row', 'col'), may hold values from -0.09375 to 0.09375
- query_rows: bfloat16 [2048, 8192], P('dep', ('row', 'col')), may hold values from -6 to 6
- key_rows: bfloat16 [2048, 8192], P('dep', ('row', 'col')), may hold values from -6 to 6
- value_rows: bfloat16 [2048, 8192], P('dep', ('row', 'col')), may hold values from -7 to 7
- seg_lengths: int32 [8], replicated, may hold values from 1 to 1536, 2048 in all
Outputs:
- grad_weight: float32 [8192, 12288], P('row', 'col')
- grad_query: bfloat16 [2048, 8192], P('dep', ('row', 'col'))
- grad_key: bfloat16 [2048, 8192], P('dep', ('row', 'col'))
- grad_value: bfloat16 [2048, 8192], P('dep', ('row', 'col'))
All inputs are finite; a program needn't handle non-finite values.
Results may differ from a plain program's by a relative error of at most 0.029.
Values may be sent and summed in bfloat16 or wider, within the bound.
No kernel may reach another device: no remote copies, remote signals or barrier semaphores. Data moves between devices by JAX's collectives and lax.ppermute only.
A program may use at most 128 MiB of HBM per device.

v0:
```python
import math
import jax
import jax.numpy as jnp
from jax import lax
from jax.sharding import Mesh
from jax.sharding import PartitionSpec as P

NEG_FILL = -1e30
FAR = 1 << 30
COL = ("zh", "x", "core")
DEP = "zl"


def segment_count(positions, seg_ends):
    return jnp.sum((positions[:, None] >= seg_ends[None, :]).astype(jnp.int32), axis=1)


def shift(x, axis, n, s):
    return lax.ppermute(x, axis, [(i, (i + s) % n) for i in range(n)])


def shift_open(x, axis, n, s):
    return lax.ppermute(x, axis, [(i, i + s) for i in range(n) if 0 <= i + s < n])


def roll_rows(x, amount, axis):
    size = x.shape[axis]
    doubled = jnp.concatenate([x, x], axis=axis)
    return lax.dynamic_slice_in_dim(doubled, (size - amount) % size, size, axis=axis)


def rolled_gather(x, axis, n, stack_axis=0):
    parts = [x] + [shift(x, axis, n, -s) for s in range(1, n)]
    return jnp.stack(parts, axis=stack_axis)


def pp_reduce_scatter(x, axis, n, dim):
    me = lax.axis_index(axis)
    acc = lax.dynamic_index_in_dim(x, me, dim, keepdims=False).astype(jnp.float32)
    for s in range(1, n):
        send = lax.dynamic_index_in_dim(x, (me + s) % n, dim, keepdims=False)
        acc = acc + shift(send, axis, n, s).astype(jnp.float32)
    return acc


def make_shards(n_zh, n_x, n_core, n_row, n_dep):

    def shards(grad_out, out_weight, query_rows, key_rows, value_rows, seg_lengths):
        n_tok, feat = (grad_out.shape[1], grad_out.shape[2])
        tok_depth = n_row * n_tok
        head_dim = query_rows.shape[1]
        inv_root = 1.0 / math.sqrt(head_dim)
        me_r = lax.axis_index("row")
        me_d = lax.axis_index(DEP)
        local = grad_out[0]
        grad_rows = rolled_gather(local, "row", n_row).reshape(tok_depth, feat)
        partial = jnp.einsum(
            "hf,tf->ht", out_weight, grad_rows, preferred_element_type=jnp.float32
        ).astype(jnp.bfloat16)
        partial = partial.reshape(n_zh, n_x, n_core, head_dim, tok_depth)
        partial = pp_reduce_scatter(partial, "core", n_core, 2).astype(jnp.bfloat16)
        partial = pp_reduce_scatter(partial, "x", n_x, 1).astype(jnp.bfloat16)
        partial = pp_reduce_scatter(partial, "zh", n_zh, 0).astype(jnp.bfloat16)
        context_grad = roll_rows(partial.T, me_r * n_tok, 0)
        kv = jnp.concatenate([key_rows, value_rows], axis=1)
        kv_all = jnp.stack(
            [kv] + [shift_open(kv, DEP, n_dep, s) for s in range(1, n_dep)], axis=0
        ).reshape(n_dep * tok_depth, 2 * head_dim)
        keys_all, values_all = (kv_all[:, :head_dim], kv_all[:, head_dim:])
        src_depth = me_d - jnp.arange(n_dep, dtype=jnp.int32)
        key_pos = (
            jnp.where(src_depth >= 0, src_depth * tok_depth, FAR)[:, None]
            + jnp.arange(tok_depth, dtype=jnp.int32)[None, :]
        ).reshape(-1)
        seg_ends = jnp.cumsum(seg_lengths)
        key_seg = segment_count(key_pos, seg_ends)
        query_pos = me_d * tok_depth + jnp.arange(tok_depth, dtype=jnp.int32)
        query_seg = segment_count(query_pos, seg_ends)
        allowed = (query_seg[:, None] == key_seg[None, :]) & (
            key_pos[None, :] <= query_pos[:, None]
        )
        scores = (
            jnp.einsum("qh,kh->qk", query_rows, keys_all, preferred_element_type=jnp.float32)
            * inv_root
        )
        masked = jnp.where(allowed, scores, NEG_FILL)
        row_max = jnp.max(masked, axis=1, keepdims=True)
        exponent = jnp.where(allowed, jnp.exp(masked - row_max), 0.0)
        row_sum = jnp.sum(exponent, axis=1, keepdims=True)
        prob_full = exponent / row_sum
        prob_half = prob_full.astype(jnp.bfloat16)
        context = jnp.dot(prob_half, values_all, preferred_element_type=jnp.float32).astype(
            jnp.bfloat16
        )
        context = roll_rows(context, -me_r * n_tok, 0)
        ctx_all = lax.all_gather(context[None], COL + (DEP,), axis=0, tiled=True)
        ctx_all = ctx_all.reshape(n_zh * n_x * n_core, n_dep * tok_depth, head_dim)
        grad_prob = jnp.dot(context_grad, values_all.T, preferred_element_type=jnp.float32)
        delta_row = jnp.sum(prob_full * grad_prob, axis=1, keepdims=True)
        grad_score = (prob_full * (grad_prob - delta_row)).astype(jnp.bfloat16)
        grad_query = (
            jnp.dot(grad_score, keys_all, preferred_element_type=jnp.float32) * inv_root
        ).astype(jnp.bfloat16)
        key_partial = (
            jnp.einsum("qk,qh->kh", grad_score, query_rows, preferred_element_type=jnp.float32)
            * inv_root
        ).astype(jnp.bfloat16)
        value_partial = jnp.einsum(
            "qk,qh->kh", prob_half, context_grad, preferred_element_type=jnp.float32
        ).astype(jnp.bfloat16)
        kv_partial = jnp.concatenate([key_partial, value_partial], axis=1).reshape(
            n_dep, tok_depth, 2 * head_dim
        )
        kv_grad = kv_partial[0].astype(jnp.float32)
        for s in range(1, n_dep):
            kv_grad = kv_grad + shift_open(kv_partial[s], DEP, n_dep, -s).astype(jnp.float32)
        kv_grad = kv_grad.astype(jnp.bfloat16)
        grad_key, grad_value = (kv_grad[:, :head_dim], kv_grad[:, head_dim:])
        by_depth = roll_rows(rolled_gather(local, DEP, n_dep), me_d, 0)
        rows_all = rolled_gather(by_depth, "row", n_row, stack_axis=1)
        rows_all = rows_all.reshape(n_dep * tok_depth, feat)
        grad_weight = jnp.einsum(
            "ntk,tf->nkf", ctx_all, rows_all, preferred_element_type=jnp.float32
        ).reshape(n_zh * n_x * n_core * head_dim, feat)
        return (grad_weight, grad_query, grad_key, grad_value)

    return shards


def solution(mesh):
    n_row, n_col, n_dep = (mesh.shape["row"], mesh.shape["col"], mesh.shape["dep"])
    n_zh, n_core = (2, 2)
    n_x = n_col // (n_zh * n_core)
    fine = Mesh(mesh.devices.reshape(n_row, n_zh, n_x, n_core, n_dep), ("row",) + COL + (DEP,))
    in_specs = (
        P("row", DEP, COL),
        P("row", COL),
        P(DEP, ("row",) + COL),
        P(DEP, ("row",) + COL),
        P(DEP, ("row",) + COL),
        P(),
    )
    out_specs = (
        P("row", COL),
        P(DEP, ("row",) + COL),
        P(DEP, ("row",) + COL),
        P(DEP, ("row",) + COL),
    )
    return jax.shard_map(
        make_shards(n_zh, n_x, n_core, n_row, n_dep),
        mesh=fine,
        in_specs=in_specs,
        out_specs=out_specs,
        check_vma=False,
    )
```

profile of v0, /device:TPU:96, one launch (start us, length us, event | category | flops | bytes accessed | tf_op | source)
XLA Modules:
  0.0 337.7 jit_solution(12385850366455091268)
XLA Ops:
  7.2 3.1 collective-permute-start.9
  11.9 7.1 %collective-permute-done.9 = bf16[128,768]{1,0:T(8,128)(2,1)S(1)} collective-permute-done((bf16[128,768]{1,0:T(8,128)(2,1)}, bf16[128,768]{1,0:T(8,128)(2,1)S(1)}, u32[]{:S(2)}, u32[]{:S(2)}) %collective-permute-start.9) | collective-permute-done | bytes 196640 | tf_op jit(solution)/shard_map/ppermute | solution.py:19
  23.8 3.1 fusion.1
  27.0 3.2 reshape.113
  30.2 6.3 %constant_dynamic-slice_fusion.1 = (bf16[2,4,1,128,512]{3,2,1,0,4:T(2,128)(2,1)}, bf16[2,4,1,128,512]{3,2,1,0,4:T(2,128)(2,1)}) fusion(bf16[2,4,2,128,512]{3,2,1,0,4:T(2,128)(2,1)S(1)} %reshape.113, s32[]{:T(128)S(6)} %select_n.93, s32[]{:T(128)S(6)} %select_n.95), kind=kLoop, calls=%fused_computation.71 | loop fusion | bytes 4194312 | tf_op jit(solution)/shard_map/jit(dynamic_index_in_dim)/dynamic_slice | solution.py:39
  36.6 6.0 %copy.34 = bf16[2,4,1,128,512]{4,3,1,0,2:T(8,128)(2,1)} copy(bf16[2,4,1,128,512]{3,2,1,0,4:T(2,128)(2,1)} %get-tuple-element.19) | data formatting | bytes 2097152
  50.3 3.1 collective-permute-done
  53.4 16.4 %collective-permute-done.1 = bf16[512,256]{1,0:T(8,128)(2,1)} collective-permute-done((bf16[512,256]{1,0:T(8,128)(2,1)S(1)}, bf16[512,256]{1,0:T(8,128)(2,1)}, u32[]{:S(2)}, u32[]{:S(2)}) %collective-permute-start.1) | collective-permute-done | bytes 262176 | tf_op jit(solution)/shard_map/ppermute | solution.py:23
  82.6 6.3 %collective-permute-done.14 = bf16[2,128,512]{2,1,0:T(8,128)(2,1)S(1)} collective-permute-done((bf16[2,128,512]{2,1,0:T(8,128)(2,1)S(1)}, bf16[2,128,512]{2,1,0:T(8,128)(2,1)S(1)}, u32[]{:S(2)}, u32[]{:S(2)}) %collective-permute-start.14) | collective-permute-done | bytes 262176 | tf_op jit(solution)/shard_map/ppermute | solution.py:19
  89.1 5.5 %collective-permute-start.16 = (bf16[128,512]{1,0:T(8,128)(2,1)S(1)}, bf16[128,512]{1,0:T(8,128)(2,1)S(1)}, u32[]{:S(2)}, u32[]{:S(2)}) collective-permute-start(bf16[128,512]{1,0:T(8,128)(2,1)S(1)} %dynamic-slice_bitcast_fusion.3), channel_id=1, source_target_pairs={{0,32},{32,0},{1,33},{33,1},{2,34},{34,2},{3,35},{35,3},{4,36},{36... | collective-permute-start | bytes 393224 | tf_op jit(solution)/shard_map/ppermute | solution.py:19
  96.3 3.9 %collective-permute-done.16 = bf16[128,512]{1,0:T(8,128)(2,1)S(1)} collective-permute-done((bf16[128,512]{1,0:T(8,128)(2,1)S(1)}, bf16[128,512]{1,0:T(8,128)(2,1)S(1)}, u32[]{:S(2)}, u32[]{:S(2)}) %collective-permute-start.16) | collective-permute-done | bytes 131104 | tf_op jit(solution)/shard_map/ppermute | solution.py:19
  100.2 4.0 %multiply_reduce_fusion = (f32[512]{0:T(512)S(1)}, f32[512,2048]{0,1:T(8,128)S(1)}, f32[512,2048]{0,1:T(8,128)}) fusion(f32[512]{0:T(512)S(1)} %fusion.4, f32[512]{0:T(512)S(1)} %get-tuple-element.28, f32[2048,512]{1,0:T(8,128)S(1)} %get-tuple-element.29, s32[512]{0:T(512)S(1)} %copy-done.13, s32[2048]{0:T(1024)S(1)} %bitcast.104, ...), kind=kOutput, calls=%fused_computation.2 | convolution fusion | flops 279182848 | bytes 13264900 | tf_op jit(solution)/shard_map/dot_general | solution.py:98
  107.6 3.7 %collective-permute-start.5 = (bf16[128,768]{1,0:T(8,128)(2,1)S(1)}, bf16[128,768]{1,0:T(8,128)(2,1)S(1)}, u32[]{:S(2)}, u32[]{:S(2)}) collective-permute-start(bf16[128,768]{1,0:T(8,128)(2,1)S(1)} %bitcast.93), channel_id=1, source_target_pairs={{0,1},{1,2},{2,3},{3,0},{4,5},{5,6},{6,7},{7,4},{8,9},{9,10},{10,1... | collective-permute-start | bytes 589832 | tf_op jit(solution)/shard_map/ppermute | solution.py:19
  111.3 4.9 %collective-permute-done.3 = bf16[128,768]{1,0:T(8,128)(2,1)S(1)} collective-permute-done((bf16[128,768]{1,0:T(8,128)(2,1)S(1)}, bf16[128,768]{1,0:T(8,128)(2,1)S(1)}, u32[]{:S(2)}, u32[]{:S(2)}) %collective-permute-start.3) | collective-permute-done | bytes 196640 | tf_op jit(solution)/shard_map/ppermute | solution.py:19
  116.2 5.0 %collective-permute-done.4 = bf16[128,768]{1,0:T(8,128)(2,1)S(1)} collective-permute-done((bf16[128,768]{1,0:T(8,128)(2,1)S(1)}, bf16[128,768]{1,0:T(8,128)(2,1)S(1)}, u32[]{:S(2)}, u32[]{:S(2)}) %collective-permute-start.4) | collective-permute-done | bytes 196640 | tf_op jit(solution)/shard_map/ppermute | solution.py:19
  123.6 18.4 %collective-permute-done.6 = bf16[4,128,768]{2,1,0:T(8,128)(2,1)S(1)} collective-permute-done((bf16[4,128,768]{2,1,0:T(8,128)(2,1)S(1)}, bf16[4,128,768]{2,1,0:T(8,128)(2,1)S(1)}, u32[]{:S(2)}, u32[]{:S(2)}) %collective-permute-start.6) | collective-permute-done | bytes 786464 | tf_op jit(solution)/shard_map/ppermute | solution.py:19
  143.9 13.0 %collective-permute-done.8 = bf16[4,128,768]{2,1,0:T(8,128)(2,1)S(1)} collective-permute-done((bf16[4,128,768]{2,1,0:T(8,128)(2,1)S(1)}, bf16[4,128,768]{2,1,0:T(8,128)(2,1)S(1)}, u32[]{:S(2)}, u32[]{:S(2)}) %collective-permute-start.8) | collective-permute-done | bytes 786464 | tf_op jit(solution)/shard_map/ppermute | solution.py:19
  163.1 7.6 %collective-permute-start.17 = (bf16[512,256]{0,1:T(8,128)(2,1)S(1)}, bf16[512,256]{0,1:T(8,128)(2,1)S(1)}, u32[]{:S(2)}, u32[]{:S(2)}) collective-permute-start(bf16[512,256]{0,1:T(8,128)(2,1)S(1)} %get-tuple-element.20), channel_id=1, source_target_pairs={{1,0},{2,1},{3,2},{5,4},{6,5},{7,6},{9,8},{10,9},{11,10},{13,12},{... | collective-permute-start | bytes 786440 | tf_op jit(solution)/shard_map/ppermute | solution.py:23
  175.1 3.9 %collective-permute-done.17 = bf16[512,256]{0,1:T(8,128)(2,1)S(1)} collective-permute-done((bf16[512,256]{0,1:T(8,128)(2,1)S(1)}, bf16[512,256]{0,1:T(8,128)(2,1)S(1)}, u32[]{:S(2)}, u32[]{:S(2)}) %collective-permute-start.17) | collective-permute-done | bytes 262176 | tf_op jit(solution)/shard_map/ppermute | solution.py:23
  179.0 7.4 %collective-permute-done.18 = bf16[512,256]{0,1:T(8,128)(2,1)S(1)} collective-permute-done((bf16[512,256]{0,1:T(8,128)(2,1)S(1)}, bf16[512,256]{0,1:T(8,128)(2,1)S(1)}, u32[]{:S(2)}, u32[]{:S(2)}) %collective-permute-start.18) | collective-permute-done | bytes 262176 | tf_op jit(solution)/shard_map/ppermute | solution.py:23
  186.3 6.2 %collective-permute-done.19 = bf16[512,256]{0,1:T(8,128)(2,1)S(1)} collective-permute-done((bf16[512,256]{0,1:T(8,128)(2,1)S(1)}, bf16[512,256]{0,1:T(8,128)(2,1)S(1)}, u32[]{:S(2)}, u32[]{:S(2)}) %collective-permute-start.19) | collective-permute-done | bytes 262176 | tf_op jit(solution)/shard_map/ppermute | solution.py:23
  194.2 112.5 %all-gather.3.cloned.1.call-done = bf16[32768,128]{1,0:T(8,128)(2,1)} async-done(((bf16[512,128]{1,0:T(8,128)(2,1)}), bf16[32768,128]{1,0:T(8,128)(2,1)}) %all-gather.3.cloned.1.call-update) | async-done | bytes 8388624 | tf_op jit(solution)/shard_map/all_gather | solution.py:96
  306.7 12.4 %copy.23 = bf16[16,2048,128]{1,2,0:T(8,128)(2,1)} copy(bf16[16,2048,128]{2,1,0:T(8,128)(2,1)} %bitcast.81) | data formatting | bytes 16777216 | tf_op jit(solution)/shard_map/reshape | solution.py:97
  319.0 11.8 %fusion.29 = f32[2048,768]{1,0:T(8,128)} fusion(bf16[2048,2048]{1,0:T(8,128)(2,1)} %bitcast.82, bf16[2048,768]{1,0:T(8,128)(2,1)} %bitcast.83), kind=kOutput, calls=%fused_computation.76 | convolution fusion | flops 6442450944 | bytes 17825792 | tf_op jit(solution)/shard_map/ntk,tf->nkf/dot_general | solution.py:122
  (99 shorter events, 48.6 us)
Async XLA Ops:
  7.2 299.5 %all-gather.3.cloned.1.call-start = ((), (), s32[]{:S(2)}) async-start(), calls=%async_computation | async-start | bytes 8519680 | tf_op jit(solution)/shard_map/all_gather | solution.py:96
  7.2 11.8 %collective-permute-start.9 = (bf16[128,768]{1,0:T(8,128)(2,1)}, bf16[128,768]{1,0:T(8,128)(2,1)S(1)}, u32[]{:S(2)}, u32[]{:S(2)}) collective-permute-start(bf16[128,768]{1,0:T(8,128)(2,1)} %bitcast.88), channel_id=1, source_target_pairs={{0,192},{64,0},{128,64},{192,128},{1,193},{65,1},{129,65},{193,129... | collective-permute-start | bytes 589832 | tf_op jit(solution)/shard_map/ppermute | solution.py:19
  10.3 9.6 %collective-permute-start.10 = (bf16[128,768]{1,0:T(8,128)(2,1)}, bf16[128,768]{1,0:T(8,128)(2,1)S(1)}, u32[]{:S(2)}, u32[]{:S(2)}) collective-permute-start(bf16[128,768]{1,0:T(8,128)(2,1)} %bitcast.89), channel_id=1, source_target_pairs={{0,128},{64,192},{128,0},{192,64},{1,129},{65,193},{129,1},{193,65... | collective-permute-start | bytes 589832 | tf_op jit(solution)/shard_map/ppermute | solution.py:19
  10.9 11.8 %collective-permute-start.11 = (bf16[128,768]{1,0:T(8,128)(2,1)}, bf16[128,768]{1,0:T(8,128)(2,1)}, u32[]{:S(2)}, u32[]{:S(2)}) collective-permute-start(bf16[128,768]{1,0:T(8,128)(2,1)} %bitcast.90), channel_id=1, source_target_pairs={{0,64},{64,128},{128,192},{192,0},{1,65},{65,129},{129,193},{193,1... | collective-permute-start | bytes 589832 | tf_op jit(solution)/shard_map/ppermute | solution.py:19
  42.5 28.6 %collective-permute-start.12 = (bf16[2,4,128,512]{3,2,1,0:T(8,128)(2,1)}, bf16[2,4,128,512]{3,2,1,0:T(8,128)(2,1)}, u32[]{:S(2)}, u32[]{:S(2)}) collective-permute-start(bf16[2,4,128,512]{3,2,1,0:T(8,128)(2,1)} %bitcast.28), channel_id=1, source_target_pairs={{0,4},{4,0},{1,5},{5,1},{2,6},{6,2},{3,7},{7,3},{8,12},{12,8},{9,1... | collective-permute-start | bytes 3145736 | tf_op jit(solution)/shard_map/ppermute | solution.py:19
  42.6 10.7 %collective-permute-start = (bf16[512,256]{1,0:T(8,128)(2,1)S(1)}, bf16[512,256]{1,0:T(8,128)(2,1)}, u32[]{:S(2)}, u32[]{:S(2)}) collective-permute-start(bf16[512,256]{1,0:T(8,128)(2,1)S(1)} %constant_dynamic-update-slice_fusion), channel_id=1, source_target_pairs={{0,1},{1,2},{2,3},{4,5},{5,6},{6,7},{8,9},{9,10},{10,11},{12,13},{... | collective-permute-start | bytes 786440 | tf_op jit(solution)/shard_map/ppermute | solution.py:23
  43.9 25.8 %collective-permute-start.1 = (bf16[512,256]{1,0:T(8,128)(2,1)S(1)}, bf16[512,256]{1,0:T(8,128)(2,1)}, u32[]{:S(2)}, u32[]{:S(2)}) collective-permute-start(bf16[512,256]{1,0:T(8,128)(2,1)S(1)} %constant_dynamic-update-slice_fusion), channel_id=1, source_target_pairs={{0,2},{1,3},{4,6},{5,7},{8,10},{9,11},{12,14},{13,15},{16,18},{17,... | collective-permute-start | bytes 786440 | tf_op jit(solution)/shard_map/ppermute | solution.py:23
  45.2 24.5 %collective-permute-start.2 = (bf16[512,256]{1,0:T(8,128)(2,1)S(1)}, bf16[512,256]{1,0:T(8,128)(2,1)}, u32[]{:S(2)}, u32[]{:S(2)}) collective-permute-start(bf16[512,256]{1,0:T(8,128)(2,1)S(1)} %constant_dynamic-update-slice_fusion), channel_id=1, source_target_pairs={{0,3},{4,7},{8,11},{12,15},{16,19},{20,23},{24,27},{28,31},{32,35}... | collective-permute-start | bytes 786440 | tf_op jit(solution)/shard_map/ppermute | solution.py:23
  46.6 23.1 %copy-start.12 = (s32[512]{0:T(512)}, s32[512]{0:T(512)S(1)}, u32[]{:S(2)}) copy-start(s32[512]{0:T(512)S(1)} %iota_add_fusion) | copy-start | bytes 6148
  71.1 33.1 %copy-start.6 = (bf16[4,512,256]{2,1,0:T(8,128)(2,1)}, bf16[4,512,256]{2,1,0:T(8,128)(2,1)S(1)}, u32[]{:S(2)}) copy-start(bf16[4,512,256]{2,1,0:T(8,128)(2,1)S(1)} %pad_maximum_fusion.1) | copy-start | bytes 3145732
  73.1 9.5 %collective-permute-start.13 = (bf16[2,128,512]{2,1,0:T(8,128)(2,1)S(1)}, bf16[2,128,512]{2,1,0:T(8,128)(2,1)S(1)}, u32[]{:S(2)}, u32[]{:S(2)}) collective-permute-start(bf16[2,128,512]{2,1,0:T(8,128)(2,1)S(1)} %get-tuple-element.23), channel_id=1, source_target_pairs={{0,8},{8,16},{16,24},{24,0},{1,9},{9,17},{17,25},{25,1},{2,10},{10... | collective-permute-start | bytes 786440 | tf_op jit(solution)/shard_map/ppermute | solution.py:19
  74.7 14.2 %collective-permute-start.14 = (bf16[2,128,512]{2,1,0:T(8,128)(2,1)S(1)}, bf16[2,128,512]{2,1,0:T(8,128)(2,1)S(1)}, u32[]{:S(2)}, u32[]{:S(2)}) collective-permute-start(bf16[2,128,512]{2,1,0:T(8,128)(2,1)S(1)} %get-tuple-element.25), channel_id=1, source_target_pairs={{0,16},{8,24},{16,0},{24,8},{1,17},{9,25},{17,1},{25,9},{2,18},{10... | collective-permute-start | bytes 786440 | tf_op jit(solution)/shard_map/ppermute | solution.py:19
  77.4 11.5 %collective-permute-start.15 = (bf16[2,128,512]{2,1,0:T(8,128)(2,1)S(1)}, bf16[2,128,512]{2,1,0:T(8,128)(2,1)S(1)}, u32[]{:S(2)}, u32[]{:S(2)}) collective-permute-start(bf16[2,128,512]{2,1,0:T(8,128)(2,1)S(1)} %get-tuple-element.24), channel_id=1, source_target_pairs={{0,24},{8,0},{16,8},{24,16},{1,25},{9,1},{17,9},{25,17},{2,26},{10... | collective-permute-start | bytes 786440 | tf_op jit(solution)/shard_map/ppermute | solution.py:19
  89.1 11.1 %collective-permute-start.16 = (bf16[128,512]{1,0:T(8,128)(2,1)S(1)}, bf16[128,512]{1,0:T(8,128)(2,1)S(1)}, u32[]{:S(2)}, u32[]{:S(2)}) collective-permute-start(bf16[128,512]{1,0:T(8,128)(2,1)S(1)} %dynamic-slice_bitcast_fusion.3), channel_id=1, source_target_pairs={{0,32},{32,0},{1,33},{33,1},{2,34},{34,2},{3,35},{35,3},{4,36},{36... | collective-permute-start | bytes 393224 | tf_op jit(solution)/shard_map/ppermute | solution.py:19
  107.4 8.8 %collective-permute-start.3 = (bf16[128,768]{1,0:T(8,128)(2,1)S(1)}, bf16[128,768]{1,0:T(8,128)(2,1)S(1)}, u32[]{:S(2)}, u32[]{:S(2)}) collective-permute-start(bf16[128,768]{1,0:T(8,128)(2,1)S(1)} %bitcast.91), channel_id=1, source_target_pairs={{0,3},{1,0},{2,1},{3,2},{4,7},{5,4},{6,5},{7,6},{8,11},{9,8},{10,9... | collective-permute-start | bytes 589832 | tf_op jit(solution)/shard_map/ppermute | solution.py:19
  107.5 13.8 %collective-permute-start.4 = (bf16[128,768]{1,0:T(8,128)(2,1)S(1)}, bf16[128,768]{1,0:T(8,128)(2,1)S(1)}, u32[]{:S(2)}, u32[]{:S(2)}) collective-permute-start(bf16[128,768]{1,0:T(8,128)(2,1)S(1)} %bitcast.92), channel_id=1, source_target_pairs={{0,2},{1,3},{2,0},{3,1},{4,6},{5,7},{6,4},{7,5},{8,10},{9,11},{10,... | collective-permute-start | bytes 589832 | tf_op jit(solution)/shard_map/ppermute | solution.py:19
  107.6 13.7 %collective-permute-start.5 = (bf16[128,768]{1,0:T(8,128)(2,1)S(1)}, bf16[128,768]{1,0:T(8,128)(2,1)S(1)}, u32[]{:S(2)}, u32[]{:S(2)}) collective-permute-start(bf16[128,768]{1,0:T(8,128)(2,1)S(1)} %bitcast.93), channel_id=1, source_target_pairs={{0,1},{1,2},{2,3},{3,0},{4,5},{5,6},{6,7},{7,4},{8,9},{9,10},{10,1... | collective-permute-start | bytes 589832 | tf_op jit(solution)/shard_map/ppermute | solution.py:19
  121.4 37.3 %copy-start.5 = (f32[512,2048]{0,1:T(8,128)S(1)}, f32[512,2048]{0,1:T(8,128)}, u32[]{:S(2)}) copy-start(f32[512,2048]{0,1:T(8,128)} %get-tuple-element.30) | copy-start | bytes 12582916
  121.5 20.6 %collective-permute-start.6 = (bf16[4,128,768]{2,1,0:T(8,128)(2,1)S(1)}, bf16[4,128,768]{2,1,0:T(8,128)(2,1)S(1)}, u32[]{:S(2)}, u32[]{:S(2)}) collective-permute-start(bf16[4,128,768]{2,1,0:T(8,128)(2,1)S(1)} %constant_dynamic-slice_fusion.2), channel_id=1, source_target_pairs={{0,192},{64,0},{128,64},{192,128},{1,193},{65,1},{129,65},{193,129... | collective-permute-start | bytes 2359304 | tf_op jit(solution)/shard_map/ppermute | solution.py:19
  121.9 22.0 %collective-permute-start.7 = (bf16[4,128,768]{2,1,0:T(8,128)(2,1)S(1)}, bf16[4,128,768]{2,1,0:T(8,128)(2,1)S(1)}, u32[]{:S(2)}, u32[]{:S(2)}) collective-permute-start(bf16[4,128,768]{2,1,0:T(8,128)(2,1)S(1)} %constant_dynamic-slice_fusion.2), channel_id=1, source_target_pairs={{0,128},{64,192},{128,0},{192,64},{1,129},{65,193},{129,1},{193,65... | collective-permute-start | bytes 2359304 | tf_op jit(solution)/shard_map/ppermute | solution.py:19
  122.4 34.5 %collective-permute-start.8 = (bf16[4,128,768]{2,1,0:T(8,128)(2,1)S(1)}, bf16[4,128,768]{2,1,0:T(8,128)(2,1)S(1)}, u32[]{:S(2)}, u32[]{:S(2)}) collective-permute-start(bf16[4,128,768]{2,1,0:T(8,128)(2,1)S(1)} %constant_dynamic-slice_fusion.2), channel_id=1, source_target_pairs={{0,64},{64,128},{128,192},{192,0},{1,65},{65,129},{129,193},{193,1... | collective-permute-start | bytes 2359304 | tf_op jit(solution)/shard_map/ppermute | solution.py:19
  163.1 15.8 %collective-permute-start.17 = (bf16[512,256]{0,1:T(8,128)(2,1)S(1)}, bf16[512,256]{0,1:T(8,128)(2,1)S(1)}, u32[]{:S(2)}, u32[]{:S(2)}) collective-permute-start(bf16[512,256]{0,1:T(8,128)(2,1)S(1)} %get-tuple-element.20), channel_id=1, source_target_pairs={{1,0},{2,1},{3,2},{5,4},{6,5},{7,6},{9,8},{10,9},{11,10},{13,12},{... | collective-permute-start | bytes 786440 | tf_op jit(solution)/shard_map/ppermute | solution.py:23
  170.7 15.6 %collective-permute-start.18 = (bf16[512,256]{0,1:T(8,128)(2,1)S(1)}, bf16[512,256]{0,1:T(8,128)(2,1)S(1)}, u32[]{:S(2)}, u32[]{:S(2)}) collective-permute-start(bf16[512,256]{0,1:T(8,128)(2,1)S(1)} %get-tuple-element.22), channel_id=1, source_target_pairs={{2,0},{3,1},{6,4},{7,5},{10,8},{11,9},{14,12},{15,13},{18,16},{19,... | collective-permute-start | bytes 786440 | tf_op jit(solution)/shard_map/ppermute | solution.py:23
  172.1 20.4 %collective-permute-start.19 = (bf16[512,256]{0,1:T(8,128)(2,1)S(1)}, bf16[512,256]{0,1:T(8,128)(2,1)S(1)}, u32[]{:S(2)}, u32[]{:S(2)}) collective-permute-start(bf16[512,256]{0,1:T(8,128)(2,1)S(1)} %get-tuple-element.21), channel_id=1, source_target_pairs={{3,0},{7,4},{11,8},{15,12},{19,16},{23,20},{27,24},{31,28},{35,32}... | collective-permute-start | bytes 786440 | tf_op jit(solution)/shard_map/ppermute | solution.py:23
  (13 other events, 108.8 us)
Sparse Core Ops, SparseCore 0:
  107.5 199.1 all-gather.2
where the time goes:
time: 338 us
  waiting for transfers between devices  216 us (64%)
  starting transfers between devices  36.3 us (11%)
  local copies, waits for them, and re-layouts  35.2 us (10%)
  matrix products  23.9 us (7%)
  between operations  14.5 us (4%)
  other arithmetic  11.6 us (3%)
    all_gather x1, waiting for transfers between devices, shards(): ctx_all = lax.all_gather(context[None], COL + (DEP,), axis=0, tiled=True)  112 us
    ppermute x14, waiting for transfers between devices, shift(): return lax.ppermute(x, axis, [(i, (i + s) % n) for i in range(n)])  66.8 us
    ppermute x6, waiting for transfers between devices, shift_open(): lax.ppermute(x, axis, [(i, i + s) for i in range(n) if 0 <= i + s < n])  36.9 us
    ppermute x14, starting transfers between devices, shift(): return lax.ppermute(x, axis, [(i, (i + s) % n) for i in range(n)])  21.9 us
    ppermute x6, starting transfers between devices, shift_open(): lax.ppermute(x, axis, [(i, i + s) for i in range(n) if 0 <= i + s < n])  14.4 us
    unnamed x45, local copies, waits for them, and re-layouts  13 us
    reshape x1, local copies, waits for them, and re-layouts, shards(): ctx_all = ctx_all.reshape(n_zh * n_x * n_core, n_dep * tok_depth, head_dim)  12.4 us
    dot_general x1, matrix products, shards(): jnp.einsum('ntk,tf->nkf', ctx_all, rows_all, preferred_element_type=jnp.f...  11.8 us
  transfers between devices with their start and end apart: 21, of which 17 were waited for; matrix products, arithmetic and copies ran while one was open for 5% of the time, Pallas kernels for 0%

commit v1 on v0

--- a/solution.py
+++ b/solution.py
@@ -93,7 +93,12 @@
             jnp.bfloat16
         )
         context = roll_rows(context, -me_r * n_tok, 0)
-        ctx_all = lax.all_gather(context[None], COL + (DEP,), axis=0, tiled=True)
+        ctx_all = jnp.concatenate(
+            lax.all_to_all(
+                jnp.stack([context[None]] * lax.axis_size(COL + (DEP,))), COL + (DEP,), 0, 0
+            ),
+            axis=0,
+        )
         ctx_all = ctx_all.reshape(n_zh * n_x * n_core, n_dep * tok_depth, head_dim)
         grad_prob = jnp.dot(context_grad, values_all.T, preferred_element_type=jnp.float32)
         delta_row = jnp.sum(prob_full * grad_prob, axis=1, keepdims=True)

time: 338 us -> 412 us (1.22)
  the two profiles are of different devices: /device:TPU:96 before, /device:TPU:1 now
where the time goes in v1:
time: 412 us; the launch traced here: 411 us
  waiting for transfers between devices  278 us (67%)
  starting transfers between devices  56.8 us (14%)
  local copies, waits for them, and re-layouts  40.3 us (10%)
  matrix products  23.9 us (6%)
  other arithmetic  11 us (3%)
    ppermute x14, waiting for transfers between devices, shift(): return lax.ppermute(x, axis, [(i, (i + s) % n) for i in range(n)])  250 us
    ppermute x6, waiting for transfers between devices, shift_open(): lax.ppermute(x, axis, [(i, i + s) for i in range(n) if 0 <= i + s < n])  27.5 us
    ppermute x14, starting transfers between devices, shift(): return lax.ppermute(x, axis, [(i, (i + s) % n) for i in range(n)])  23.8 us
    all_to_all x1, starting transfers between devices, shards(): lax.all_to_all(jnp.stack([context[None]] * lax.axis_size(COL + (DEP,))),...  17.9 us
    ppermute x6, starting transfers between devices, shift_open(): lax.ppermute(x, axis, [(i, i + s) for i in range(n) if 0 <= i + s < n])  15 us
    unnamed x45, local copies, waits for them, and re-layouts  12.9 us
    dot_general x1, local copies, waits for them, and re-layouts, shards(): jnp.einsum('ntk,tf->nkf', ctx_all, rows_all, preferred_element_type=jnp.f...  12.3 us
    dot_general x1, matrix products, shards(): jnp.einsum('ntk,tf->nkf', ctx_all, rows_all, preferred_element_type=jnp.f...  11.8 us
  transfers between devices with their start and end apart: 21, of which 14 were waited for; matrix products, arithmetic and copies ran while one was open for 4% of the time, Pallas kernels for 0%

profile of v1, /device:TPU:1, one launch (start us, length us, event | category | flops | bytes accessed | tf_op | source)
XLA Modules:
  0.0 411.0 jit_solution(14538623817890356671)
XLA Ops:
  2.9 2.6 collective-permute-start.10
  7.6 6.6 %collective-permute-done.10 = bf16[128,768]{1,0:T(8,128)(2,1)S(1)} collective-permute-done((bf16[128,768]{1,0:T(8,128)(2,1)}, bf16[128,768]{1,0:T(8,128)(2,1)S(1)}, u32[]{:S(2)}, u32[]{:S(2)}) %collective-permute-start.10) | collective-permute-done | bytes 196640 | tf_op jit(solution)/shard_map/ppermute | solution.py:19
  15.3 3.1 fusion.1
  18.5 3.2 reshape.111
  21.7 6.3 %constant_dynamic-slice_fusion.1 = (bf16[2,4,1,128,512]{3,2,1,0,4:T(2,128)(2,1)}, bf16[2,4,1,128,512]{3,2,1,0,4:T(2,128)(2,1)}) fusion(bf16[2,4,2,128,512]{3,2,1,0,4:T(2,128)(2,1)S(1)} %reshape.111, s32[]{:T(128)S(6)} %select_n.93, s32[]{:T(128)S(6)} %select_n.95), kind=kLoop, calls=%fused_computation.71 | loop fusion | bytes 4194312 | tf_op jit(solution)/shard_map/jit(dynamic_index_in_dim)/dynamic_slice | solution.py:39
  28.1 6.0 %copy.51 = bf16[2,4,1,128,512]{4,3,1,0,2:T(8,128)(2,1)} copy(bf16[2,4,1,128,512]{3,2,1,0,4:T(2,128)(2,1)} %get-tuple-element.27) | data formatting | bytes 2097152
  35.7 7.0 %collective-permute-start.2 = (bf16[512,256]{1,0:T(8,128)(2,1)S(1)}, bf16[512,256]{1,0:T(8,128)(2,1)}, u32[]{:S(2)}, u32[]{:S(2)}) collective-permute-start(bf16[512,256]{1,0:T(8,128)(2,1)S(1)} %constant_dynamic-update-slice_fusion), channel_id=1, source_target_pairs={{0,3},{4,7},{8,11},{12,15},{16,19},{20,23},{24,27},{28,31},{32,35}... | collective-permute-start | bytes 786440 | tf_op jit(solution)/shard_map/ppermute | solution.py:23
  50.6 2.8 collective-permute-done.1
  53.4 5.6 %collective-permute-done = bf16[512,256]{1,0:T(8,128)(2,1)} collective-permute-done((bf16[512,256]{1,0:T(8,128)(2,1)S(1)}, bf16[512,256]{1,0:T(8,128)(2,1)}, u32[]{:S(2)}, u32[]{:S(2)}) %collective-permute-start) | collective-permute-done | bytes 262176 | tf_op jit(solution)/shard_map/ppermute | solution.py:23
  67.6 3.0 collective-permute-done.13
  70.6 6.6 %collective-permute-done.14 = bf16[2,128,512]{2,1,0:T(8,128)(2,1)S(1)} collective-permute-done((bf16[2,128,512]{2,1,0:T(8,128)(2,1)S(1)}, bf16[2,128,512]{2,1,0:T(8,128)(2,1)S(1)}, u32[]{:S(2)}, u32[]{:S(2)}) %collective-permute-start.14) | collective-permute-done | bytes 262176 | tf_op jit(solution)/shard_map/ppermute | solution.py:19
  77.4 4.3 %collective-permute-start.16 = (bf16[128,512]{1,0:T(8,128)(2,1)S(1)}, bf16[128,512]{1,0:T(8,128)(2,1)S(1)}, u32[]{:S(2)}, u32[]{:S(2)}) collective-permute-start(bf16[128,512]{1,0:T(8,128)(2,1)S(1)} %dynamic-slice_bitcast_fusion.3), channel_id=1, source_target_pairs={{0,32},{32,0},{1,33},{33,1},{2,34},{34,2},{3,35},{35,3},{4,36},{36... | collective-permute-start | bytes 393224 | tf_op jit(solution)/shard_map/ppermute | solution.py:19
  85.2 4.0 multiply_reduce_fusion
  91.7 5.2 %stack.60 = bf16[64,1,512,128]{3,2,1,0:T(8,128)(2,1)} broadcast(bf16[512,128]{1,0:T(8,128)(2,1)S(1)} %fusion.24), dimensions={2,3} | broadcast | bytes 8519680 | tf_op jit(solution)/shard_map/stack | solution.py:98
  96.9 17.9 %all-to-all-start = ((bf16[64,1,512,128]{3,2,1,0:T(8,128)(2,1)}), bf16[64,1,512,128]{3,2,1,0:T(8,128)(2,1)}, u32[]{:S(2)}, u32[]{:S(2)}) async-start(bf16[64,1,512,128]{3,2,1,0:T(8,128)(2,1)} %stack.60), calls=%async_computation | async-start | bytes 16777216 | tf_op jit(solution)/shard_map/all_to_all | solution.py:97
  114.9 3.3 collective-permute-start.3
  118.7 182.6 %collective-permute-done.3 = bf16[128,768]{1,0:T(8,128)(2,1)S(1)} collective-permute-done((bf16[128,768]{1,0:T(8,128)(2,1)S(1)}, bf16[128,768]{1,0:T(8,128)(2,1)S(1)}, u32[]{:S(2)}, u32[]{:S(2)}) %collective-permute-start.3) | collective-permute-done | bytes 196640 | tf_op jit(solution)/shard_map/ppermute | solution.py:19
  301.3 15.0 %collective-permute-done.4 = bf16[128,768]{1,0:T(8,128)(2,1)S(1)} collective-permute-done((bf16[128,768]{1,0:T(8,128)(2,1)S(1)}, bf16[128,768]{1,0:T(8,128)(2,1)S(1)}, u32[]{:S(2)}, u32[]{:S(2)}) %collective-permute-start.4) | collective-permute-done | bytes 196640 | tf_op jit(solution)/shard_map/ppermute | solution.py:19
  320.6 15.8 %collective-permute-done.7 = bf16[4,128,768]{2,1,0:T(8,128)(2,1)S(1)} collective-permute-done((bf16[4,128,768]{2,1,0:T(8,128)(2,1)S(1)}, bf16[4,128,768]{2,1,0:T(8,128)(2,1)S(1)}, u32[]{:S(2)}, u32[]{:S(2)}) %collective-permute-start.7) | collective-permute-done | bytes 786464 | tf_op jit(solution)/shard_map/ppermute | solution.py:19
  336.4 16.7 %collective-permute-done.6 = bf16[4,128,768]{2,1,0:T(8,128)(2,1)S(1)} collective-permute-done((bf16[4,128,768]{2,1,0:T(8,128)(2,1)S(1)}, bf16[4,128,768]{2,1,0:T(8,128)(2,1)S(1)}, u32[]{:S(2)}, u32[]{:S(2)}) %collective-permute-start.6) | collective-permute-done | bytes 786464 | tf_op jit(solution)/shard_map/ppermute | solution.py:19
  366.1 10.6 %collective-permute-done.17 = bf16[512,256]{0,1:T(8,128)(2,1)S(1)} collective-permute-done((bf16[512,256]{0,1:T(8,128)(2,1)S(1)}, bf16[512,256]{0,1:T(8,128)(2,1)S(1)}, u32[]{:S(2)}, u32[]{:S(2)}) %collective-permute-start.17) | collective-permute-done | bytes 262176 | tf_op jit(solution)/shard_map/ppermute | solution.py:23
  376.7 8.5 %collective-permute-done.18 = bf16[512,256]{0,1:T(8,128)(2,1)S(1)} collective-permute-done((bf16[512,256]{0,1:T(8,128)(2,1)S(1)}, bf16[512,256]{0,1:T(8,128)(2,1)S(1)}, u32[]{:S(2)}, u32[]{:S(2)}) %collective-permute-start.18) | collective-permute-done | bytes 262176 | tf_op jit(solution)/shard_map/ppermute | solution.py:23
  386.9 12.3 %copy.40 = bf16[16,128,2048]{2,1,0:T(8,128)(2,1)} copy(bf16[16,128,2048]{1,2,0:T(8,128)(2,1)} %bitcast.9) | data formatting | bytes 16777216 | tf_op jit(solution)/shard_map/ntk,tf->nkf/dot_general | solution.py:127
  399.2 11.8 %fusion.29 = f32[2048,768]{1,0:T(8,128)} fusion(bf16[2048,2048]{1,0:T(8,128)(2,1)} %bitcast.81, bf16[2048,768]{1,0:T(8,128)(2,1)} %bitcast.82), kind=kOutput, calls=%fused_computation.76 | convolution fusion | flops 6442450944 | bytes 17825792 | tf_op jit(solution)/shard_map/ntk,tf->nkf/dot_general | solution.py:127
  (99 shorter events, 49.1 us)
Async XLA Ops:
  0.6 6.9 %collective-permute-start.11 = (bf16[128,768]{1,0:T(8,128)(2,1)}, bf16[128,768]{1,0:T(8,128)(2,1)S(1)}, u32[]{:S(2)}, u32[]{:S(2)}) collective-permute-start(bf16[128,768]{1,0:T(8,128)(2,1)} %bitcast.87), channel_id=1, source_target_pairs={{0,64},{64,128},{128,192},{192,0},{1,65},{65,129},{129,193},{193,1... | collective-permute-start | bytes 589832 | tf_op jit(solution)/shard_map/ppermute | solution.py:19
  2.9 11.3 %collective-permute-start.10 = (bf16[128,768]{1,0:T(8,128)(2,1)}, bf16[128,768]{1,0:T(8,128)(2,1)S(1)}, u32[]{:S(2)}, u32[]{:S(2)}) collective-permute-start(bf16[128,768]{1,0:T(8,128)(2,1)} %bitcast.88), channel_id=1, source_target_pairs={{0,128},{64,192},{128,0},{192,64},{1,129},{65,193},{129,1},{193,65... | collective-permute-start | bytes 589832 | tf_op jit(solution)/shard_map/ppermute | solution.py:19
  5.5 8.7 %collective-permute-start.9 = (bf16[128,768]{1,0:T(8,128)(2,1)}, bf16[128,768]{1,0:T(8,128)(2,1)}, u32[]{:S(2)}, u32[]{:S(2)}) collective-permute-start(bf16[128,768]{1,0:T(8,128)(2,1)} %bitcast.89), channel_id=1, source_target_pairs={{0,192},{64,0},{128,64},{192,128},{1,193},{65,1},{129,65},{193,129... | collective-permute-start | bytes 589832 | tf_op jit(solution)/shard_map/ppermute | solution.py:19
  28.1 19.9 %copy-start.4 = (bf16[2,4,1,128,512]{3,2,1,0,4:T(2,128)(2,1)S(1)}, bf16[2,4,1,128,512]{3,2,1,0,4:T(2,128)(2,1)}, u32[]{:S(2)}) copy-start(bf16[2,4,1,128,512]{3,2,1,0,4:T(2,128)(2,1)} %get-tuple-element.26) | copy-start | bytes 3145732
  34.1 26.2 %collective-permute-start.12 = (bf16[2,4,128,512]{3,2,1,0:T(8,128)(2,1)}, bf16[2,4,128,512]{3,2,1,0:T(8,128)(2,1)}, u32[]{:S(2)}, u32[]{:S(2)}) collective-permute-start(bf16[2,4,128,512]{3,2,1,0:T(8,128)(2,1)} %bitcast.28), channel_id=1, source_target_pairs={{0,4},{4,0},{1,5},{5,1},{2,6},{6,2},{3,7},{7,3},{8,12},{12,8},{9,1... | collective-permute-start | bytes 3145736 | tf_op jit(solution)/shard_map/ppermute | solution.py:19
  35.7 14.9 %collective-permute-start.2 = (bf16[512,256]{1,0:T(8,128)(2,1)S(1)}, bf16[512,256]{1,0:T(8,128)(2,1)}, u32[]{:S(2)}, u32[]{:S(2)}) collective-permute-start(bf16[512,256]{1,0:T(8,128)(2,1)S(1)} %constant_dynamic-update-slice_fusion), channel_id=1, source_target_pairs={{0,3},{4,7},{8,11},{12,15},{16,19},{20,23},{24,27},{28,31},{32,35}... | collective-permute-start | bytes 786440 | tf_op jit(solution)/shard_map/ppermute | solution.py:23
  42.7 10.7 %collective-permute-start.1 = (bf16[512,256]{1,0:T(8,128)(2,1)S(1)}, bf16[512,256]{1,0:T(8,128)(2,1)}, u32[]{:S(2)}, u32[]{:S(2)}) collective-permute-start(bf16[512,256]{1,0:T(8,128)(2,1)S(1)} %constant_dynamic-update-slice_fusion), channel_id=1, source_target_pairs={{0,2},{1,3},{4,6},{5,7},{8,10},{9,11},{12,14},{13,15},{16,18},{17,... | collective-permute-start | bytes 786440 | tf_op jit(solution)/shard_map/ppermute | solution.py:23
  44.6 14.3 %collective-permute-start = (bf16[512,256]{1,0:T(8,128)(2,1)S(1)}, bf16[512,256]{1,0:T(8,128)(2,1)}, u32[]{:S(2)}, u32[]{:S(2)}) collective-permute-start(bf16[512,256]{1,0:T(8,128)(2,1)S(1)} %constant_dynamic-update-slice_fusion), channel_id=1, source_target_pairs={{0,1},{1,2},{2,3},{4,5},{5,6},{6,7},{8,9},{9,10},{10,11},{12,13},{... | collective-permute-start | bytes 786440 | tf_op jit(solution)/shard_map/ppermute | solution.py:23
  60.3 29.0 %copy-start.6 = (bf16[4,512,256]{2,1,0:T(8,128)(2,1)}, bf16[4,512,256]{2,1,0:T(8,128)(2,1)S(1)}, u32[]{:S(2)}) copy-start(bf16[4,512,256]{2,1,0:T(8,128)(2,1)S(1)} %pad_maximum_fusion.1) | copy-start | bytes 3145732
  62.3 8.3 %collective-permute-start.13 = (bf16[2,128,512]{2,1,0:T(8,128)(2,1)S(1)}, bf16[2,128,512]{2,1,0:T(8,128)(2,1)S(1)}, u32[]{:S(2)}, u32[]{:S(2)}) collective-permute-start(bf16[2,128,512]{2,1,0:T(8,128)(2,1)S(1)} %get-tuple-element.31), channel_id=1, source_target_pairs={{0,8},{8,16},{16,24},{24,0},{1,9},{9,17},{17,25},{25,1},{2,10},{10... | collective-permute-start | bytes 786440 | tf_op jit(solution)/shard_map/ppermute | solution.py:19
  63.6 7.1 %collective-permute-start.15 = (bf16[2,128,512]{2,1,0:T(8,128)(2,1)S(1)}, bf16[2,128,512]{2,1,0:T(8,128)(2,1)S(1)}, u32[]{:S(2)}, u32[]{:S(2)}) collective-permute-start(bf16[2,128,512]{2,1,0:T(8,128)(2,1)S(1)} %get-tuple-element.32), channel_id=1, source_target_pairs={{0,24},{8,0},{16,8},{24,16},{1,25},{9,1},{17,9},{25,17},{2,26},{10... | collective-permute-start | bytes 786440 | tf_op jit(solution)/shard_map/ppermute | solution.py:19
  65.0 12.2 %collective-permute-start.14 = (bf16[2,128,512]{2,1,0:T(8,128)(2,1)S(1)}, bf16[2,128,512]{2,1,0:T(8,128)(2,1)S(1)}, u32[]{:S(2)}, u32[]{:S(2)}) collective-permute-start(bf16[2,128,512]{2,1,0:T(8,128)(2,1)S(1)} %get-tuple-element.33), channel_id=1, source_target_pairs={{0,16},{8,24},{16,0},{24,8},{1,17},{9,25},{17,1},{25,9},{2,18},{10... | collective-permute-start | bytes 786440 | tf_op jit(solution)/shard_map/ppermute | solution.py:19
  77.4 7.8 %collective-permute-start.16 = (bf16[128,512]{1,0:T(8,128)(2,1)S(1)}, bf16[128,512]{1,0:T(8,128)(2,1)S(1)}, u32[]{:S(2)}, u32[]{:S(2)}) collective-permute-start(bf16[128,512]{1,0:T(8,128)(2,1)S(1)} %dynamic-slice_bitcast_fusion.3), channel_id=1, source_target_pairs={{0,32},{32,0},{1,33},{33,1},{2,34},{34,2},{3,35},{35,3},{4,36},{36... | collective-permute-start | bytes 393224 | tf_op jit(solution)/shard_map/ppermute | solution.py:19
  96.9 290.0 %all-to-all-start = ((bf16[64,1,512,128]{3,2,1,0:T(8,128)(2,1)}), bf16[64,1,512,128]{3,2,1,0:T(8,128)(2,1)}, u32[]{:S(2)}, u32[]{:S(2)}) async-start(bf16[64,1,512,128]{3,2,1,0:T(8,128)(2,1)} %stack.60), calls=%async_computation | async-start | bytes 16777216 | tf_op jit(solution)/shard_map/all_to_all | solution.py:97
  114.9 186.4 %collective-permute-start.3 = (bf16[128,768]{1,0:T(8,128)(2,1)S(1)}, bf16[128,768]{1,0:T(8,128)(2,1)S(1)}, u32[]{:S(2)}, u32[]{:S(2)}) collective-permute-start(bf16[128,768]{1,0:T(8,128)(2,1)S(1)} %bitcast.90), channel_id=1, source_target_pairs={{0,3},{1,0},{2,1},{3,2},{4,7},{5,4},{6,5},{7,6},{8,11},{9,8},{10,9... | collective-permute-start | bytes 589832 | tf_op jit(solution)/shard_map/ppermute | solution.py:19
  118.1 198.2 %collective-permute-start.5 = (bf16[128,768]{1,0:T(8,128)(2,1)S(1)}, bf16[128,768]{1,0:T(8,128)(2,1)S(1)}, u32[]{:S(2)}, u32[]{:S(2)}) collective-permute-start(bf16[128,768]{1,0:T(8,128)(2,1)S(1)} %bitcast.91), channel_id=1, source_target_pairs={{0,1},{1,2},{2,3},{3,0},{4,5},{5,6},{6,7},{7,4},{8,9},{9,10},{10,1... | collective-permute-start | bytes 589832 | tf_op jit(solution)/shard_map/ppermute | solution.py:19
  118.1 198.2 %collective-permute-start.4 = (bf16[128,768]{1,0:T(8,128)(2,1)S(1)}, bf16[128,768]{1,0:T(8,128)(2,1)S(1)}, u32[]{:S(2)}, u32[]{:S(2)}) collective-permute-start(bf16[128,768]{1,0:T(8,128)(2,1)S(1)} %bitcast.92), channel_id=1, source_target_pairs={{0,2},{1,3},{2,0},{3,1},{4,6},{5,7},{6,4},{7,5},{8,10},{9,11},{10,... | collective-permute-start | bytes 589832 | tf_op jit(solution)/shard_map/ppermute | solution.py:19
  316.5 39.9 %copy-start.5 = (f32[512,2048]{0,1:T(8,128)S(1)}, f32[512,2048]{0,1:T(8,128)}, u32[]{:S(2)}) copy-start(f32[512,2048]{0,1:T(8,128)} %get-tuple-element.38) | copy-start | bytes 12582916
  316.6 19.8 %collective-permute-start.7 = (bf16[4,128,768]{2,1,0:T(8,128)(2,1)S(1)}, bf16[4,128,768]{2,1,0:T(8,128)(2,1)S(1)}, u32[]{:S(2)}, u32[]{:S(2)}) collective-permute-start(bf16[4,128,768]{2,1,0:T(8,128)(2,1)S(1)} %constant_dynamic-slice_fusion.2), channel_id=1, source_target_pairs={{0,128},{64,192},{128,0},{192,64},{1,129},{65,193},{129,1},{193,65... | collective-permute-start | bytes 2359304 | tf_op jit(solution)/shard_map/ppermute | solution.py:19
  319.1 34.0 %collective-permute-start.6 = (bf16[4,128,768]{2,1,0:T(8,128)(2,1)S(1)}, bf16[4,128,768]{2,1,0:T(8,128)(2,1)S(1)}, u32[]{:S(2)}, u32[]{:S(2)}) collective-permute-start(bf16[4,128,768]{2,1,0:T(8,128)(2,1)S(1)} %constant_dynamic-slice_fusion.2), channel_id=1, source_target_pairs={{0,192},{64,0},{128,64},{192,128},{1,193},{65,1},{129,65},{193,129... | collective-permute-start | bytes 2359304 | tf_op jit(solution)/shard_map/ppermute | solution.py:19
  320.1 34.4 %collective-permute-start.8 = (bf16[4,128,768]{2,1,0:T(8,128)(2,1)S(1)}, bf16[4,128,768]{2,1,0:T(8,128)(2,1)S(1)}, u32[]{:S(2)}, u32[]{:S(2)}) collective-permute-start(bf16[4,128,768]{2,1,0:T(8,128)(2,1)S(1)} %constant_dynamic-slice_fusion.2), channel_id=1, source_target_pairs={{0,64},{64,128},{128,192},{192,0},{1,65},{65,129},{129,193},{193,1... | collective-permute-start | bytes 2359304 | tf_op jit(solution)/shard_map/ppermute | solution.py:19
  360.8 15.9 %collective-permute-start.17 = (bf16[512,256]{0,1:T(8,128)(2,1)S(1)}, bf16[512,256]{0,1:T(8,128)(2,1)S(1)}, u32[]{:S(2)}, u32[]{:S(2)}) collective-permute-start(bf16[512,256]{0,1:T(8,128)(2,1)S(1)} %get-tuple-element.28), channel_id=1, source_target_pairs={{1,0},{2,1},{3,2},{5,4},{6,5},{7,6},{9,8},{10,9},{11,10},{13,12},{... | collective-permute-start | bytes 786440 | tf_op jit(solution)/shard_map/ppermute | solution.py:23
  362.1 14.7 %collective-permute-start.19 = (bf16[512,256]{0,1:T(8,128)(2,1)S(1)}, bf16[512,256]{0,1:T(8,128)(2,1)S(1)}, u32[]{:S(2)}, u32[]{:S(2)}) collective-permute-start(bf16[512,256]{0,1:T(8,128)(2,1)S(1)} %get-tuple-element.29), channel_id=1, source_target_pairs={{3,0},{7,4},{11,8},{15,12},{19,16},{23,20},{27,24},{31,28},{35,32}... | collective-permute-start | bytes 786440 | tf_op jit(solution)/shard_map/ppermute | solution.py:23
  363.4 21.9 %collective-permute-start.18 = (bf16[512,256]{0,1:T(8,128)(2,1)S(1)}, bf16[512,256]{0,1:T(8,128)(2,1)S(1)}, u32[]{:S(2)}, u32[]{:S(2)}) collective-permute-start(bf16[512,256]{0,1:T(8,128)(2,1)S(1)} %get-tuple-element.30), channel_id=1, source_target_pairs={{2,0},{3,1},{6,4},{7,5},{10,8},{11,9},{14,12},{15,13},{18,16},{19,... | collective-permute-start | bytes 786440 | tf_op jit(solution)/shard_map/ppermute | solution.py:23
  (13 other events, 123.4 us)
